TPU v7x, 32 devices: a whole 2x2x4 slice. The times are simulated.
32 devices in a mesh: ctx: 8 (over z, y), grp: 4 (over x, core).
Axes of the slice: x: 2, y: 2, z: 4, core: 2. Of those that a mesh axis runs over, the one named last changes fastest.
Arguments:
- query: bfloat16 [1024, 12288], P('ctx', 'grp')
- land_keys: bfloat16 [32, 768], P('ctx')
- land_values: bfloat16 [32, 512], P('ctx'), may hold values from -6 to 6
- d_out: bfloat16 [1024, 8192], P('ctx', 'grp'), may hold values from -6 to 6
- doc_start: int32 [1024], P('ctx'), may hold values from 0 to 1023, as said below
Outputs:
- branch_out: bfloat16 [1024, 8192], P('ctx', 'grp')
- d_query: float32 [1024, 12288], P('ctx', 'grp')
- d_keys: float32 [32, 768], P('ctx')
- d_values: float32 [32, 512], P('ctx')
Inputs may be any that keep to these rules, and one draw needn't show every extreme that they name: doc_start never decreases from one position to the next, doc_start[t] <= t, a document starts at position 0, and one starts at the last position.
All inputs are finite; a program needn't handle non-finite values.
Results may differ from a plain program's by a relative error of at most 0.0049.
Values may be sent and summed in bfloat16 or wider, within the bound.
No kernel may reach another device: no remote copies, remote signals or barrier semaphores. Data moves between devices by JAX's collectives and lax.ppermute only.
A program may use at most 64 MiB of HBM per device.

v0:
```python
import math

import jax
import jax.numpy as jnp
from jax import lax
from jax.sharding import PartitionSpec as P

KVG = 4
DK = 192
DV = 128
BLK = 32


def shards(query, land_keys, land_values, d_out, doc_start):
    tok_rows = query.shape[0]
    head_count = query.shape[1] // DK
    nl_local = land_keys.shape[0]
    score_scale = 1.0 / math.sqrt(DK)
    group_id = lax.axis_index("grp") // (lax.axis_size("grp") // KVG)
    group_keys = lax.dynamic_slice_in_dim(land_keys, group_id * DK, DK, 1)
    group_values = lax.dynamic_slice_in_dim(land_values, group_id * DV, DV, 1)
    queries = query.reshape(tok_rows, head_count, DK)
    grads_in = d_out.reshape(tok_rows, head_count, DV)
    ctx_index = lax.axis_index("ctx")
    positions = ctx_index * tok_rows + jnp.arange(tok_rows, dtype=jnp.int32)
    keys_whole, values_whole = (
        lax.all_gather(group_keys, "ctx", axis=0, tiled=True),
        lax.all_gather(group_values, "ctx", axis=0, tiled=True),
    )
    columns = jnp.arange(keys_whole.shape[0], dtype=jnp.int32)
    allowed = (columns[None, :] * BLK >= doc_start[:, None]) & (
        (columns[None, :] + 1) * BLK <= positions[:, None] + 1
    )
    scores = (
        jnp.einsum("thd,jd->thj", queries, keys_whole, preferred_element_type=jnp.float32)
        * score_scale
    )
    masked, allowed = (jnp.where(allowed[:, None, :], scores, -1e30), allowed[:, None, :])
    peak = jnp.maximum(jnp.max(masked, axis=2), 0.0)
    expo = jnp.where(allowed, jnp.exp(masked - peak[..., None]), 0.0)
    denom = jnp.exp(-peak) + jnp.sum(expo, axis=2)
    weight = expo / denom[..., None]
    weight_b = weight.astype(jnp.bfloat16)
    context = jnp.einsum("thj,je->the", weight_b, values_whole, preferred_element_type=jnp.float32)
    branch_out = context.astype(jnp.bfloat16).reshape(tok_rows, head_count * DV)
    delta = jnp.sum(grads_in.astype(jnp.float32) * context, axis=2)
    d_weight = jnp.einsum("the,je->thj", grads_in, values_whole, preferred_element_type=jnp.float32)
    d_score_b = (weight * (d_weight - delta[..., None])).astype(jnp.bfloat16)
    d_query = (
        jnp.einsum("thj,jd->thd", d_score_b, keys_whole, preferred_element_type=jnp.float32)
        * score_scale
    ).reshape(tok_rows, head_count * DK)
    key_grad = (
        jnp.einsum("thj,thd->jd", d_score_b, queries, preferred_element_type=jnp.float32)
        * score_scale
    )
    value_grad = jnp.einsum("thj,the->je", weight_b, grads_in, preferred_element_type=jnp.float32)
    owned = lax.psum_scatter(
        jnp.concatenate([key_grad, value_grad], axis=1), "ctx", scatter_dimension=0, tiled=True
    )
    slots = (jnp.arange(KVG, dtype=jnp.int32) == group_id).astype(jnp.float32)
    placed = owned[:, None, :] * slots[None, :, None]
    totals = lax.psum(placed, "grp")
    d_keys = totals[:, :, :DK].reshape(nl_local, KVG * DK)
    d_values = totals[:, :, DK:].reshape(nl_local, KVG * DV)
    return (branch_out, d_query, d_keys, d_values)


def solution(mesh):
    return jax.shard_map(
        shards,
        mesh=mesh,
        in_specs=(P("ctx", "grp"), P("ctx", None), P("ctx", None), P("ctx", "grp"), P("ctx")),
        out_specs=(P("ctx", "grp"), P("ctx", "grp"), P("ctx", None), P("ctx", None)),
        check_vma=False,
    )
```

profile of v0, /device:TPU:0, one launch (start us, length us, event | category | flops | bytes accessed | tf_op | source)
XLA Modules:
  0.0 104.1 jit_solution(3525271043548078328)
XLA Ops:
  0.6 0.0 copy-start
  0.6 0.0 copy-start.1
  0.7 1.3 %dynamic-slice = u32[1]{0:T(128)} dynamic-slice(u32[32]{0:T(128)} %constant.50, u32[]{:T(128)S(6)} %add.60), dynamic_slice_sizes={1} | dynamic-slice | bytes 12
  2.7 0.7 dynamic-slice_bitcast_fusion.1
  3.3 0.0 copy-done
  3.3 0.1 dynamic-slice_bitcast_fusion
  3.4 0.7 compare_and_fusion
  4.2 22.3 %all-gather.1 = bf16[8,4,128]{2,1,0:T(4,128)(2,1)S(1)} all-gather(bf16[1,4,128]{2,1,0:T(4,128)(2,1)S(1)} %dynamic-slice_bitcast_fusion.1), channel_id=1, replica_groups=mesh['ctx'=8,'grp'=4] {'ctx'}, dimensions={0}, use_global_device_ids=true | all-gather | bytes 9216 | tf_op jit(solution)/shard_map/all_gather | solution.py:28
  26.5 26.1 %all-gather = bf16[8,4,192]{2,1,0:T(4,128)(2,1)S(1)} all-gather(bf16[1,4,192]{2,1,0:T(4,128)(2,1)S(1)} %dynamic-slice_bitcast_fusion), channel_id=1, replica_groups=mesh['ctx'=8,'grp'=4] {'ctx'}, dimensions={0}, use_global_device_ids=true | all-gather | bytes 13824 | tf_op jit(solution)/shard_map/all_gather | solution.py:27
  52.6 1.3 %copy.23 = bf16[128,2048]{0,1:T(8,128)(2,1)S(1)} copy(bf16[128,2048]{1,0:T(8,128)(2,1)} %param.8) | data formatting | bytes 1048576 | tf_op args[3]
  53.9 0.0 copy-done.1
  53.9 0.4 copy.22
  54.3 0.3 fusion.13
  54.6 0.1 fusion.7
  54.7 0.3 convolution_bitcast_fusion.1
  55.0 0.4 multiply_reduce_fusion
  55.3 0.2 fusion.4
  55.6 0.3 fusion.5
  55.9 0.1 pad_maximum_fusion
  56.0 33.4 %all-reduce = f32[32,320]{1,0:T(8,128)S(1)} all-reduce(f32[32,320]{1,0:T(8,128)S(1)} %pad_maximum_fusion), channel_id=2, replica_groups=mesh['ctx'=8,'grp'=4] {'ctx'}, use_global_device_ids=true, to_apply=%region_3.4.clone | all-reduce | flops 10240 | bytes 81920
  89.4 1.0 copy.26
  90.4 0.1 broadcast_multiply_fusion
  90.5 10.3 %psum.7 = f32[4,4,320]{2,1,0:T(4,128)S(1)} all-reduce(f32[4,4,320]{2,1,0:T(4,128)S(1)} %broadcast_multiply_fusion), channel_id=1, replica_groups=mesh['ctx'=8,'grp'=4] {'grp'}, use_global_device_ids=true, to_apply=%region_4.5 | all-reduce | flops 5120 | bytes 40960 | tf_op jit(solution)/shard_map/psum | solution.py:63
  100.7 0.1 slice_bitcast_fusion
  100.8 0.7 reshape.112
  101.5 0.6 copy.32
  102.1 0.4 convolution_multiply_fusion
  102.5 1.6 %copy.27 = f32[128,3072]{1,0:T(8,128)} copy(f32[128,3072]{0,1:T(8,128)S(1)} %bitcast.46) | data formatting | bytes 3145728
  (8 shorter events, 0.1 us)
Async XLA Ops:
  0.6 2.7 %copy-start = (bf16[4,768]{1,0:T(4,128)(2,1)S(1)}, bf16[4,768]{1,0:T(4,128)(2,1)}, u32[]{:S(2)}) copy-start(bf16[4,768]{1,0:T(4,128)(2,1)} %param.6) | copy-start | bytes 18436
  0.6 53.3 %copy-start.1 = (bf16[128,3072]{1,0:T(8,128)(2,1)S(1)}, bf16[128,3072]{1,0:T(8,128)(2,1)}, u32[]{:S(2)}) copy-start(bf16[128,3072]{1,0:T(8,128)(2,1)} %param.5) | copy-start | bytes 2359300
where the time goes:
time: 104 us
  blocking collectives  92 us (88%)
  local copies, waits for them, and re-layouts  7.81 us (8%)
  matrix products  1.87 us (2%)
  between operations  1.44 us (1%)
    unnamed x1, blocking collectives  33.4 us
    all_gather x1, blocking collectives, shards(): lax.all_gather(group_keys, 'ctx', axis=0, tiled=True)  26.1 us
    all_gather x1, blocking collectives, shards(): lax.all_gather(group_values, 'ctx', axis=0, tiled=True)  22.3 us
    psum x1, blocking collectives, shards(): totals = lax.psum(placed, 'grp')  10.3 us
    unnamed x15, local copies, waits for them, and re-layouts  7.12 us

commit v1 on v0

--- a/solution.py
+++ b/solution.py
@@ -11,22 +11,31 @@
 BLK = 32
 
 
+def gather_ctx(block):
+    n = lax.axis_size("ctx")
+    if n & (n - 1):
+        return lax.all_gather(block, "ctx", axis=0, tiled=True)
+    copies = jnp.broadcast_to(block[None], (n,) + block.shape)
+    return lax.all_to_all(copies, "ctx", 0, 0, tiled=False).reshape(n * block.shape[0], block.shape[1])
+
+
 def shards(query, land_keys, land_values, d_out, doc_start):
     tok_rows = query.shape[0]
     head_count = query.shape[1] // DK
     nl_local = land_keys.shape[0]
+    n_ctx = lax.axis_size("ctx")
+    n_grp = lax.axis_size("grp")
+    per_group = n_grp // KVG
     score_scale = 1.0 / math.sqrt(DK)
-    group_id = lax.axis_index("grp") // (lax.axis_size("grp") // KVG)
+    group_id = lax.axis_index("grp") // per_group
     group_keys = lax.dynamic_slice_in_dim(land_keys, group_id * DK, DK, 1)
     group_values = lax.dynamic_slice_in_dim(land_values, group_id * DV, DV, 1)
     queries = query.reshape(tok_rows, head_count, DK)
     grads_in = d_out.reshape(tok_rows, head_count, DV)
     ctx_index = lax.axis_index("ctx")
     positions = ctx_index * tok_rows + jnp.arange(tok_rows, dtype=jnp.int32)
-    keys_whole, values_whole = (
-        lax.all_gather(group_keys, "ctx", axis=0, tiled=True),
-        lax.all_gather(group_values, "ctx", axis=0, tiled=True),
-    )
+    landmarks = gather_ctx(jnp.concatenate([group_keys, group_values], axis=1))
+    keys_whole, values_whole = landmarks[:, :DK], landmarks[:, DK:]
     columns = jnp.arange(keys_whole.shape[0], dtype=jnp.int32)
     allowed = (columns[None, :] * BLK >= doc_start[:, None]) & (
         (columns[None, :] + 1) * BLK <= positions[:, None] + 1
@@ -55,12 +64,13 @@
         * score_scale
     )
     value_grad = jnp.einsum("thj,the->je", weight_b, grads_in, preferred_element_type=jnp.float32)
-    owned = lax.psum_scatter(
-        jnp.concatenate([key_grad, value_grad], axis=1), "ctx", scatter_dimension=0, tiled=True
+    partial = jnp.concatenate([key_grad, value_grad], axis=1).reshape(1, n_ctx, nl_local, DK + DV)
+    outgoing = jnp.broadcast_to(partial, (n_grp, n_ctx, nl_local, DK + DV)).reshape(
+        n_grp * n_ctx, nl_local, DK + DV
     )
-    slots = (jnp.arange(KVG, dtype=jnp.int32) == group_id).astype(jnp.float32)
-    placed = owned[:, None, :] * slots[None, :, None]
-    totals = lax.psum(placed, "grp")
+    incoming = lax.all_to_all(outgoing, ("grp", "ctx"), 0, 0, tiled=False)
+    totals = incoming.reshape(KVG, per_group, n_ctx, nl_local, DK + DV).sum(axis=(1, 2))
+    totals = jnp.transpose(totals, (1, 0, 2))
     d_keys = totals[:, :, :DK].reshape(nl_local, KVG * DK)
     d_values = totals[:, :, DK:].reshape(nl_local, KVG * DV)
     return (branch_out, d_query, d_keys, d_values)

time: 104 us -> 31.2 us (0.30)
  blocking collectives: 92 us -> 0 us
  starting transfers between devices: 0 us -> 9.89 us
  waiting for transfers between devices: 0 us -> 9.37 us
    all_gather x2 -> x0, blocking collectives: 48.4 us -> none  [the longest x1 26.1 us: shards(): lax.all_gather(group_keys, 'ctx', axis=0, tiled=True)]
    unnamed x1 -> x0, blocking collectives: 33.4 us -> none
    psum x1 -> x0, blocking collectives: 10.3 us -> none  [shards(): totals = lax.psum(placed, 'grp')]
    all_to_all x0 -> x2, starting transfers between devices: none -> 9.89 us  [the longest x1 7.31 us: gather_ctx(): lax.all_to_all(copies, 'ctx', 0, 0, tiled=False)]
    all_to_all x0 -> x2, waiting for transfers between devices: none -> 9.37 us  [the longest x1 5.2 us: shards(): incoming = lax.all_to_all(outgoing, ('grp', 'ctx'), 0, 0, tiled=False)]
    unnamed x15 -> x8, local copies, waits for them, and re-layouts: 7.12 us -> 4.33 us
    broadcast_in_dim x0 -> x3, local copies, waits for them, and re-layouts: none -> 1.34 us  [the longest x2 0.72 us: shards(): jnp.broadcast_to(partial, (n_grp, n_ctx, nl_local, DK + DV))]
  transfers between devices with their start and end apart: 0 -> 2, of which waited for: 0 -> 2; matrix products, arithmetic and copies ran while one was open for 0% -> 18% of each run, Pallas kernels for 0% -> 0%
where the time goes in v1:
time: 31.2 us; the launch traced here: 30.9 us
  starting transfers between devices  9.89 us (32%)
  waiting for transfers between devices  9.37 us (30%)
  local copies, waits for them, and re-layouts  7.9 us (25%)
  matrix products  1.98 us (6%)
  other arithmetic  1.01 us (3%)
  between operations  0.78 us (2%)
    all_to_all x1, starting transfers between devices, gather_ctx(): lax.all_to_all(copies, 'ctx', 0, 0, tiled=False)  7.31 us
    all_to_all x1, waiting for transfers between devices, shards(): incoming = lax.all_to_all(outgoing, ('grp', 'ctx'), 0, 0, tiled=False)  5.2 us
    unnamed x8, local copies, waits for them, and re-layouts  4.33 us
    all_to_all x1, waiting for transfers between devices, gather_ctx(): lax.all_to_all(copies, 'ctx', 0, 0, tiled=False)  4.16 us
    all_to_all x1, starting transfers between devices, shards(): incoming = lax.all_to_all(outgoing, ('grp', 'ctx'), 0, 0, tiled=False)  2.58 us
    dynamic_slice x1, local copies, waits for them, and re-layouts, shards(): group_values = lax.dynamic_slice_in_dim(land_values, group_id * DV, DV, 1)  0.76 us
    and x1, other arithmetic, shards(): (columns[None, :] * BLK >= doc_start[:, None]) & ((columns[None, :] + 1)...  0.73 us
    broadcast_in_dim x2, local copies, waits for them, and re-layouts, shards(): jnp.broadcast_to(partial, (n_grp, n_ctx, nl_local, DK + DV))  0.72 us
  transfers between devices with their start and end apart: 2, of which 2 were waited for; matrix products, arithmetic and copies ran while one was open for 18% of the time, Pallas kernels for 0%

profile of v1, /device:TPU:0, one launch (start us, length us, event | category | flops | bytes accessed | tf_op | source)
XLA Modules:
  0.0 30.9 jit_solution(5771682893396405526)
XLA Ops:
  0.6 0.0 copy-start
  0.6 0.0 copy-start.1
  0.7 0.8 %constant_dynamic-slice_fusion = bf16[4,128]{1,0:T(4,128)(2,1)S(1)} fusion(bf16[4,512]{1,0:T(4,128)(2,1)} %param.7, s32[]{:T(128)S(6)} %select_n.17), kind=kLoop, calls=%fused_computation.27 | loop fusion | bytes 2052 | tf_op jit(solution)/shard_map/dynamic_slice | solution.py:32
  1.4 0.0 copy-done
  1.4 0.1 constant_dynamic-slice_fusion.1
  1.5 0.1 pad_maximum_fusion.1
  1.6 0.6 %broadcast_in_dim.41 = bf16[8,4,320]{2,1,0:T(4,128)(2,1)} broadcast(bf16[4,320]{1,0:T(4,128)(2,1)S(1)} %pad_maximum_fusion.1), dimensions={1,2} | broadcast | bytes 23040 | tf_op jit(solution)/shard_map/broadcast_in_dim | solution.py:18
  2.2 7.3 %all-to-all-start = ((bf16[8,4,320]{2,1,0:T(4,128)(2,1)}), bf16[8,4,320]{2,1,0:T(4,128)(2,1)S(1)}, u32[]{:S(2)}, u32[]{:S(2)}) async-start(bf16[8,4,320]{2,1,0:T(4,128)(2,1)} %broadcast_in_dim.41), calls=%async_computation | async-start | bytes 49152 | tf_op jit(solution)/shard_map/all_to_all | solution.py:19
  9.5 0.7 %compare_and_fusion = pred[128,32]{0,1:T(8,128)(4,1)S(1)} fusion(s32[128]{0:T(128)S(1)} %add_add_fusion, s32[128]{0:T(128)} %param.9, s32[32]{0:T(128)S(1)} %get-tuple-element.29, s32[32]{0:T(128)S(1)} %get-tuple-element.30), kind=kLoop, calls=%fused_computation.21 | loop fusion | flops 12288 | bytes 5376 | tf_op jit(solution)/shard_map/and | solution.py:40
  10.3 1.3 %copy.38 = bf16[128,2048]{0,1:T(8,128)(2,1)S(1)} copy(bf16[128,2048]{1,0:T(8,128)(2,1)} %param.8) | data formatting | bytes 1048576 | tf_op args[3]
  11.6 0.0 copy-done.1
  11.6 0.4 %copy.37 = bf16[128,3072]{0,1:T(8,128)(2,1)S(1)} copy(bf16[128,3072]{1,0:T(8,128)(2,1)S(1)} %copy-done.1) | data formatting | bytes 1572864 | tf_op args[0]
  12.0 4.2 %all-to-all-done = bf16[8,4,320]{2,1,0:T(4,128)(2,1)S(1)} async-done(((bf16[8,4,320]{2,1,0:T(4,128)(2,1)}), bf16[8,4,320]{2,1,0:T(4,128)(2,1)S(1)}, u32[]{:S(2)}, u32[]{:S(2)}) %all-to-all-start) | async-done | bytes 20512 | tf_op jit(solution)/shard_map/all_to_all | solution.py:19
  16.2 0.3 fusion.13
  16.4 0.1 fusion.7
  16.5 0.4 %multiply_reduce_fusion = (f32[128,16]{0,1:T(8,128)S(1)}, bf16[128,16,128]{0,2,1:T(8,128)(2,1)S(1)}) fusion(bf16[128,2048]{0,1:T(8,128)(2,1)S(1)} %copy.38, bf16[32,320]{1,0:T(8,128)(2,1)S(1)} %reshape.115, f32[128,16]{0,1:T(8,128)S(1)} %exponential_add_fusion, f32[128,16,32]{0,2,1:T(8,128)S(1)} %get-tuple-element.27, ...), kind=kOutput, calls=%fused_computation.11 | convolution fusion | flops 18085888 | bytes 1347584 | tf_op jit(solution)/shard_map/thj,je->the/dot_general | solution.py:53
  17.0 0.3 convolution_bitcast_fusion.1
  17.3 0.3 fusion.4
  17.5 0.3 %fusion.5 = f32[32,192]{1,0:T(8,128)S(1)} fusion(bf16[128,16,32]{0,2,1:T(8,128)(2,1)S(1)} %fusion.4, bf16[128,16,192]{0,2,1:T(8,128)(2,1)S(1)} %bitcast.46), kind=kOutput, calls=%fused_computation.9 | convolution fusion | flops 25171968 | bytes 942080 | tf_op jit(solution)/shard_map/thj,thd->jd/dot_general | solution.py:63
  17.9 0.1 pad_maximum_fusion
  18.0 0.7 %broadcast_in_dim.45 = f32[4,8,4,320]{3,2,1,0:T(4,128)} broadcast(f32[8,4,320]{2,1,0:T(4,128)S(1)} %broadcast_in_dim.44), dimensions={1,2,3} | broadcast | bytes 204800 | tf_op jit(solution)/shard_map/broadcast_in_dim | solution.py:68
  18.7 2.6 %all-to-all-start.1 = ((f32[32,4,320]{2,1,0:T(4,128)}), f32[32,4,320]{2,1,0:T(4,128)S(1)}, u32[]{:S(2)}, u32[]{:S(2)}) async-start(f32[32,4,320]{2,1,0:T(4,128)} %bitcast.10), calls=%async_computation.1 | async-start | bytes 393216 | tf_op jit(solution)/shard_map/all_to_all | solution.py:71
  21.3 1.0 %copy.44 = bf16[128,2048]{1,0:T(8,128)(2,1)} copy(bf16[128,2048]{0,1:T(8,128)(2,1)S(1)} %bitcast.48) | data formatting | bytes 1048576
  22.3 0.4 %convolution_multiply_fusion = f32[128,16,192]{0,2,1:T(8,128)S(1)} fusion(bf16[128,16,32]{0,2,1:T(8,128)(2,1)S(1)} %fusion.4, bf16[32,320]{1,0:T(8,128)(2,1)S(1)} %reshape.115), kind=kOutput, calls=%fused_computation | convolution fusion | flops 25559040 | bytes 1720320 | tf_op jit(solution)/shard_map/thj,jd->thd/dot_general | solution.py:59
  22.7 1.6 %copy.45 = f32[128,3072]{1,0:T(8,128)} copy(f32[128,3072]{0,1:T(8,128)S(1)} %bitcast.47) | data formatting | bytes 3145728
  24.3 5.2 %all-to-all-done.1 = f32[32,4,320]{2,1,0:T(4,128)S(1)} async-done(((f32[32,4,320]{2,1,0:T(4,128)}), f32[32,4,320]{2,1,0:T(4,128)S(1)}, u32[]{:S(2)}, u32[]{:S(2)}) %all-to-all-start.1) | async-done | bytes 163872 | tf_op jit(solution)/shard_map/all_to_all | solution.py:71
  29.6 0.7 %slice_bitcast_fusion.3 = f32[4,512]{1,0:T(4,128)} fusion(f32[4,4,320]{2,0,1:T(4,128)S(1)} %bitcast.51), kind=kLoop, calls=%fused_computation.22 | loop fusion | bytes 16384 | tf_op jit(solution)/shard_map/reshape | solution.py:75
  30.2 0.7 %reshape.122 = f32[4,768]{1,0:T(4,128)} reshape(f32[4,4,192]{2,1,0:T(4,128)S(1)} %copy.43) | data formatting | bytes 24576 | tf_op jit(solution)/shard_map/reshape | solution.py:74
  (9 shorter events, 0.1 us)
Async XLA Ops:
  0.6 0.8 %copy-start = (bf16[4,768]{1,0:T(4,128)(2,1)S(1)}, bf16[4,768]{1,0:T(4,128)(2,1)}, u32[]{:S(2)}) copy-start(bf16[4,768]{1,0:T(4,128)(2,1)} %param.6) | copy-start | bytes 18436
  0.6 10.9 %copy-start.1 = (bf16[128,3072]{1,0:T(8,128)(2,1)S(1)}, bf16[128,3072]{1,0:T(8,128)(2,1)}, u32[]{:S(2)}) copy-start(bf16[128,3072]{1,0:T(8,128)(2,1)} %param.5) | copy-start | bytes 2359300
  2.2 13.9 %all-to-all-start = ((bf16[8,4,320]{2,1,0:T(4,128)(2,1)}), bf16[8,4,320]{2,1,0:T(4,128)(2,1)S(1)}, u32[]{:S(2)}, u32[]{:S(2)}) async-start(bf16[8,4,320]{2,1,0:T(4,128)(2,1)} %broadcast_in_dim.41), calls=%async_computation | async-start | bytes 49152 | tf_op jit(solution)/shard_map/all_to_all | solution.py:19
  18.7 10.8 %all-to-all-start.1 = ((f32[32,4,320]{2,1,0:T(4,128)}), f32[32,4,320]{2,1,0:T(4,128)S(1)}, u32[]{:S(2)}, u32[]{:S(2)}) async-start(f32[32,4,320]{2,1,0:T(4,128)} %bitcast.10), calls=%async_computation.1 | async-start | bytes 393216 | tf_op jit(solution)/shard_map/all_to_all | solution.py:71
